TPU v7x, 128 devices: a whole 4x4x4 slice. The times are simulated.
128 devices in a mesh: req: 16 (over y, z), head: 8 (over x, core).
Axes of the slice: x: 4, y: 4, z: 4, core: 2. Of those that a mesh axis runs over, the one named last changes fastest.
Arguments:
- hidden_in: bfloat16 [16384, 2048], P('req'), may hold values from -6 to 6
- cache_latent: bfloat16 [16, 512, 512], P('req'), may hold values from -6 to 6
- cache_rope: bfloat16 [16, 512, 64], P('req')
- cache_lengths: int32 [16], P('req'), may hold values from 32 to 512, as said below
- attn_gain: float32 [2048], replicated, may hold values from 0.25 to 1.75
- w_query: bfloat16 [2048, 3072], P(None, 'head'), may hold values from -0.125 to 0.125
- w_latent: bfloat16 [2048, 512], replicated, may hold values from -0.125 to 0.125
- w_latent_rope: bfloat16 [2048, 64], replicated, may hold values from -0.125 to 0.125
- latent_gain: float32 [512], replicated, may hold values from 0.25 to 1.75
- w_key_up: bfloat16 [512, 2048], P(None, 'head'), may hold values from -0.25 to 0.25
- w_value_up: bfloat16 [512, 2048], P(None, 'head'), may hold values from -2 to 2
- w_out: bfloat16 [2048, 2048], P('head'), may hold values from -0.375 to 0.375
- post_gain: float32 [2048], replicated, may hold values from 0.1 to 1.9
- w_router: bfloat16 [2048, 64], replicated
- routes: int32 [16384, 6], P(('req', 'head')), may hold values from 0 to 63, all different within a row; in each aligned block of 128 rows (0 to 127, 128 to 255, ...) at most 14 rows name the same one
- shared_gate: bfloat16 [2048, 2816], P(None, 'head'), may hold values from -0.125 to 0.125
- shared_up: bfloat16 [2048, 2816], P(None, 'head'), may hold values from -0.125 to 0.125
- shared_down: bfloat16 [2816, 2048], P('head')
- expert_gate: bfloat16 [128, 2048, 704], P(('req', 'head')), may hold values from -0.125 to 0.125
- expert_up: bfloat16 [128, 2048, 704], P(('req', 'head')), may hold values from -0.125 to 0.125
- expert_down: bfloat16 [128, 704, 2048], P(('req', 'head')), may hold values from -0.875 to 0.875
Outputs:
- layer_out: bfloat16 [16384, 2048], P(('req', 'head'))
Inputs may be any that keep to these rules, and one draw needn't show every extreme that they name: `cache_lengths`: two requests have exactly 512 cached rows; each other request has between 32 and 64. `routes`: the 6 experts of a row differ; within each aligned block of 128 rows (the rows of one device) no expert is named more than 14 times.
All inputs are finite; a program needn't handle non-finite values.
Results may differ from a plain program's by a relative error of at most 0.025.
The roundings to bfloat16 on the way count: a program that leaves them out, or rounds other values in their place, can miss the bound.
Values may be sent and summed in bfloat16 or wider, within the bound.
No kernel may reach another device: no remote copies, remote signals or barrier semaphores. Data moves between devices by JAX's collectives and lax.ppermute only.
A program may use at most 192 MiB of HBM per device.

v0:
```python
import math

import jax
import jax.numpy as jnp
from jax import lax
from jax.sharding import PartitionSpec as P

NOPE = 128
ROPE = 64
VDIM = 128
LATENT = 512
EXPERTS = 64
CAP = 14


def rms_scale(values, gain_row):
    return values * lax.rsqrt(jnp.mean(values * values, axis=-1, keepdims=True) + 1e-06) * gain_row


def rotate(values, positions):
    half_size = values.shape[-1] // 2
    frequency = jnp.exp(
        jnp.arange(half_size, dtype=jnp.float32) * (-2.0 * math.log(10000.0) / values.shape[-1])
    )
    angles = positions.astype(jnp.float32)[:, None] * frequency[None, :]
    shape_mid = (angles.shape[0],) + (1,) * (values.ndim - 2) + (half_size,)
    cosine = jnp.cos(angles).reshape(shape_mid)
    sine_part = jnp.sin(angles).reshape(shape_mid)
    first_half = values[..., :half_size]
    second_half = values[..., half_size:]
    return jnp.concatenate(
        [
            first_half * cosine - second_half * sine_part,
            second_half * cosine + first_half * sine_part,
        ],
        axis=-1,
    )


def attend_rows(
    absorbed, query_rope, first_row, cache_lat, cache_keys, length, new_latent, new_rope, block_rows
):
    query_count = absorbed.shape[0]
    head_count = absorbed.shape[1]
    latent_width = absorbed.shape[2]
    score_scale = (NOPE + ROPE) ** (-0.5)

    def update(state_now, keys_latent, keys_rope, visible):
        row_max, row_total, weighted = state_now
        scores = (
            jnp.einsum("qhl,kl->qhk", absorbed, keys_latent, preferred_element_type=jnp.float32)
            + jnp.einsum("qhr,kr->qhk", query_rope, keys_rope, preferred_element_type=jnp.float32)
        ) * score_scale
        scores = jnp.where(visible, scores, -jnp.inf)
        new_max = jnp.maximum(row_max, jnp.max(scores, axis=-1))
        exponent = jnp.exp(scores - new_max[..., None])
        factor = jnp.exp(row_max - new_max)
        row_total = row_total * factor + jnp.sum(exponent, axis=-1)
        weighted = weighted * factor[..., None] + jnp.einsum(
            "qhk,kl->qhl",
            exponent.astype(jnp.bfloat16),
            keys_latent,
            preferred_element_type=jnp.float32,
        )
        return (new_max, row_total, weighted)

    initial = (
        jnp.full((query_count, head_count), -jnp.inf, jnp.float32),
        jnp.zeros((query_count, head_count), jnp.float32),
        jnp.zeros((query_count, head_count, latent_width), jnp.float32),
    )
    cache_block = min(128, cache_lat.shape[0])
    block_total = (length + cache_block - 1) // cache_block

    def cache_step(block_index, state_now):
        start_row = block_index * cache_block
        keys_latent = lax.dynamic_slice_in_dim(cache_lat, start_row, cache_block, 0)
        keys_rope = lax.dynamic_slice_in_dim(cache_keys, start_row, cache_block, 0)
        visible = (start_row + jnp.arange(cache_block, dtype=jnp.int32) < length)[None, None, :]
        return update(state_now, keys_latent, keys_rope, visible)

    state_now = lax.fori_loop(0, block_total, cache_step, initial)
    query_pos = first_row + jnp.arange(query_count, dtype=jnp.int32)
    for key_block in range(first_row // block_rows + 1):
        key_start = key_block * block_rows
        visible = (key_start + jnp.arange(block_rows, dtype=jnp.int32))[None, None, :] <= query_pos[
            :, None, None
        ]
        state_now = update(
            state_now,
            new_latent[key_start : key_start + block_rows],
            new_rope[key_start : key_start + block_rows],
            visible,
        )
    row_max, row_total, weighted = state_now
    return (weighted / row_total[..., None]).astype(jnp.bfloat16)


def per_device(
    hidden_in,
    cache_latent,
    cache_rope,
    cache_lengths,
    attn_gain,
    w_query,
    w_latent,
    w_latent_rope,
    latent_gain,
    w_key_up,
    w_value_up,
    w_out,
    post_gain,
    w_router,
    routes,
    shared_gate,
    shared_up,
    shared_down,
    expert_gate,
    expert_up,
    expert_down,
):
    request_rows = hidden_in.shape[0]
    model_width = hidden_in.shape[1]
    row_count = routes.shape[0]
    top_count = routes.shape[1]
    head_local = w_query.shape[1] // (NOPE + ROPE)
    length = cache_lengths[0]
    head_index = lax.axis_index("head")
    normed_in = rms_scale(hidden_in.astype(jnp.float32), attn_gain).astype(jnp.bfloat16)
    positions = length + jnp.arange(request_rows, dtype=jnp.int32)
    query_all = jnp.dot(normed_in, w_query, preferred_element_type=jnp.float32).reshape(
        request_rows, head_local, NOPE + ROPE
    )
    query_nope = query_all[..., :NOPE].astype(jnp.bfloat16)
    query_rope = rotate(query_all[..., NOPE:], positions).astype(jnp.bfloat16)
    own_start = head_index * row_count
    own_in = lax.dynamic_slice_in_dim(normed_in, own_start, row_count, 0)
    own_positions = length + own_start + jnp.arange(row_count, dtype=jnp.int32)
    own_latent = rms_scale(
        jnp.dot(own_in, w_latent, preferred_element_type=jnp.float32), latent_gain
    ).astype(jnp.bfloat16)
    own_rope = rotate(
        jnp.dot(own_in, w_latent_rope, preferred_element_type=jnp.float32), own_positions
    ).astype(jnp.bfloat16)
    new_latent, new_rope = (
        lax.all_gather(own_latent, "head", axis=0, tiled=True),
        lax.all_gather(own_rope, "head", axis=0, tiled=True),
    )
    key_up = w_key_up.reshape(LATENT, head_local, NOPE)
    absorbed = jnp.einsum(
        "chn,lhn->chl", query_nope, key_up, preferred_element_type=jnp.float32
    ).astype(jnp.bfloat16)
    value_up = w_value_up.reshape(LATENT, head_local, VDIM)
    block_rows = min(512, request_rows)
    outputs = []
    for first_row in range(0, request_rows, block_rows):
        latent_out = attend_rows(
            absorbed[first_row : first_row + block_rows],
            query_rope[first_row : first_row + block_rows],
            first_row,
            cache_latent[0],
            cache_rope[0],
            length,
            new_latent,
            new_rope,
            block_rows,
        )
        head_out = jnp.einsum(
            "qhl,lhv->qhv", latent_out, value_up, preferred_element_type=jnp.float32
        ).astype(jnp.bfloat16)
        outputs.append(head_out.reshape(block_rows, head_local * VDIM))
    head_rows = jnp.concatenate(outputs, axis=0)
    attn_term = jnp.dot(head_rows, w_out, preferred_element_type=jnp.float32)
    attn_sum = lax.psum(attn_term.astype(jnp.bfloat16), "head").astype(jnp.float32)
    residual = (hidden_in.astype(jnp.float32) + attn_sum).astype(jnp.bfloat16)
    normed = rms_scale(residual.astype(jnp.float32), post_gain).astype(jnp.bfloat16)
    shared_act = (
        jax.nn.silu(jnp.dot(normed, shared_gate, preferred_element_type=jnp.float32))
        * jnp.dot(normed, shared_up, preferred_element_type=jnp.float32)
    ).astype(jnp.bfloat16)
    shared_own = lax.psum_scatter(
        jnp.dot(shared_act, shared_down, preferred_element_type=jnp.float32).astype(jnp.bfloat16),
        "head",
        scatter_dimension=0,
        tiled=True,
    ).astype(jnp.float32)
    residual_own = lax.dynamic_slice_in_dim(residual, own_start, row_count, 0)
    normed_own = lax.dynamic_slice_in_dim(normed, own_start, row_count, 0)
    experts = EXPERTS
    capacity = CAP
    devices = lax.axis_size("req") * lax.axis_size("head")
    split_count = max(1, devices // experts)
    local_count = max(1, experts // devices)
    group_count = devices // split_count
    slot_width = local_count * capacity
    logits = jnp.dot(normed_own, w_router, preferred_element_type=jnp.float32)
    matches = routes[:, :, None] == jnp.arange(experts, dtype=jnp.int32)[None, None, :]
    chosen = jnp.sum(jnp.where(matches, logits[:, None, :], 0.0), axis=-1)
    route_weight = jax.nn.softmax(chosen, axis=-1)
    pair_hits = matches.reshape(row_count * top_count, experts).astype(jnp.int32)
    pair_ranks = jnp.cumsum(pair_hits, axis=0) - pair_hits
    slot_of = jnp.sum(pair_ranks * pair_hits, axis=-1)
    target = routes.reshape(-1) * capacity + slot_of
    slot_token = (
        jnp.full((experts * capacity,), row_count, jnp.int32)
        .at[target]
        .set(jnp.arange(row_count * top_count, dtype=jnp.int32) // top_count)
    )
    padded = jnp.concatenate([normed_own, jnp.zeros((1, model_width), jnp.bfloat16)], axis=0)
    send_rows = padded[slot_token]
    outgoing = jnp.repeat(
        send_rows.reshape(group_count, slot_width, model_width), split_count, axis=0
    )
    arrived = lax.all_to_all(outgoing, ("req", "head"), split_axis=0, concat_axis=0, tiled=True)
    received = arrived.reshape(devices, local_count, capacity, model_width)
    gate_values = jnp.einsum(
        "pjcd,jdf->pjcf", received, expert_gate, preferred_element_type=jnp.float32
    )
    upward = jnp.einsum("pjcd,jdf->pjcf", received, expert_up, preferred_element_type=jnp.float32)
    activation = (jax.nn.silu(gate_values) * upward).astype(jnp.bfloat16)
    partial_value = jnp.einsum(
        "pjcf,jfd->pjcd", activation, expert_down, preferred_element_type=jnp.float32
    ).reshape(devices, slot_width, model_width)
    returned = lax.all_to_all(
        partial_value.astype(jnp.bfloat16), ("req", "head"), split_axis=0, concat_axis=0, tiled=True
    ).astype(partial_value.dtype)
    expert_rows = (
        jnp.sum(returned.reshape(group_count, split_count, slot_width, model_width), axis=1)
        .reshape(experts * capacity, model_width)
        .astype(jnp.bfloat16)
    )
    picked = expert_rows[target].reshape(row_count, top_count, model_width)
    routed = jnp.sum(route_weight[:, :, None] * picked, axis=1)
    return (residual_own.astype(jnp.float32) + shared_own + routed).astype(jnp.bfloat16)


def solution(mesh):
    in_specs = (
        P("req", None),
        P("req", None, None),
        P("req", None, None),
        P("req"),
        P(),
        P(None, "head"),
        P(),
        P(),
        P(),
        P(None, "head"),
        P(None, "head"),
        P("head", None),
        P(),
        P(),
        P(("req", "head"), None),
        P(None, "head"),
        P(None, "head"),
        P("head", None),
        P(("req", "head"), None, None),
        P(("req", "head"), None, None),
        P(("req", "head"), None, None),
    )
    out_specs = P(("req", "head"), None)
    return jax.shard_map(
        per_device, mesh=mesh, in_specs=in_specs, out_specs=out_specs, check_vma=False
    )
```

profile of v0, /device:TPU:10, one launch (start us, length us, event | category | flops | bytes accessed | tf_op | source)
XLA Modules:
  0.0 570.3 jit_solution(3553800194016890410)
XLA Ops:
  6.5 3.2 fusion.37
  9.8 3.4 fusion.39
  13.2 1.9 copy-done.9
  17.3 4.5 fusion.131
  23.0 1.3 copy-done.7
  24.3 1.5 fusion.127
  26.3 1.1 subtract_convert_fusion
  28.1 1.7 broadcast.272.clone.1
  29.8 6.1 %while.28 = (s32[]{:T(128)}, f32[512,2]{0,1:T(2,128)S(1)}, f32[512,2]{0,1:T(2,128)S(1)}, f32[512,2,512]{2,0,1:T(8,128)}, s32[]{:T(128)}, /*index=5*/s32[]{:T(128...) while((s32[]{:T(128)}, f32[512,2]{0,1:T(2,128)S(1)}, ...), condition=%wide.region_4.5_spmd, body=%wide.region_1.4_spmd.sunk | while | flops 287312128 | bytes 25117568 | solution.py:82
  29.8 0.8 add_compare_fusion.4
  30.6 1.2 fusion.177
  31.8 1.7 fusion.178
  33.6 0.8 multiply_add_fusion.11
  34.5 1.4 copy-done.4
  35.9 1.6 broadcast.272.clone
  37.5 5.8 %while.29 = (s32[]{:T(128)}, f32[512,2]{0,1:T(2,128)S(1)}, f32[512,2]{0,1:T(2,128)S(1)}, f32[512,2,512]{2,0,1:T(8,128)}, s32[]{:T(128)}, /*index=5*/s32[]{:T(128...) while((s32[]{:T(128)}, f32[512,2]{0,1:T(2,128)S(1)}, ...), condition=%wide.region_11.12_spmd, body=%wide.region_8.11_spmd.sunk | while | flops 287312128 | bytes 25117568 | solution.py:82
  37.5 0.8 add_compare_fusion.5
  38.3 1.0 fusion.185
  39.2 1.7 fusion.186
  41.1 0.8 multiply_add_fusion.13
  42.0 1.3 copy-done.2
  43.3 1.4 fusion.85
  44.7 1.1 copy.108
  46.6 23.3 %all_gather.7 = bf16[1024,64]{0,1:T(8,128)(2,1)S(1)} all-gather(bf16[128,64]{0,1:T(8,128)(2,1)S(1)} %pad_maximum_fusion.1), channel_id=1, replica_groups=mesh['req'=16,'head'=8] {'head'}, dimensions={0}, use_global_device_ids=true | all-gather | bytes 147456 | tf_op jit(solution)/shard_map/all_gather | solution.py:147
  70.7 1.1 broadcast_compare_fusion
  71.7 1.8 fusion.98
  73.6 1.8 fusion.97
  75.4 1.8 fusion.96
  77.2 3.1 fusion.130
  80.6 1.0 copy-done.15
  81.6 1.0 copy-done.8
  82.6 0.9 fusion.129
  84.2 0.9 fusion.128
  86.5 2.1 fusion.67
  88.6 3.6 fusion.64
  92.1 4.3 fusion.63
  96.4 4.5 convolution_convert_fusion.2
  102.3 1.8 reduce-window.6
  104.5 3.4 scatter_custom_fusion
  108.0 97.3 %all-reduce.3.cloned.1.call-done = bf16[1024,2048]{1,0:T(8,128)(2,1)} async-done(((bf16[1024,2048]{1,0:T(8,128)(2,1)}), bf16[1024,2048]{1,0:T(8,128)(2,1)}) %all-reduce.3.cloned.1.call-update) | async-done | bytes 4194320 | tf_op jit(solution)/shard_map/psum | solution.py:174
  205.2 5.5 fusion.34
  210.7 1.0 fusion.36
  211.8 0.9 copy-done.5
  212.7 1.9 copy-done.11
  215.4 5.0 gather_fusion
  220.5 6.0 %reshape.326 = bf16[64,14,2048]{2,1,0:T(8,128)(2,1)} reshape(bf16[896,2048]{1,0:T(8,128)(2,1)} %gather_fusion) | data formatting | bytes 7340032 | tf_op jit(solution)/shard_map/reshape | solution.py:212
  226.5 6.8 %broadcast_in_dim.112 = bf16[64,2,14,2048]{3,2,1,0:T(8,128)(2,1)} broadcast(bf16[64,14,2048]{2,1,0:T(8,128)(2,1)} %reshape.326), dimensions={0,2,3} | broadcast | bytes 11010048 | tf_op jit(solution)/shard_map/broadcast_in_dim | solution.py:211
  233.2 11.3 %all-to-all-start = ((bf16[128,14,2048]{2,1,0:T(8,128)(2,1)}), bf16[128,14,2048]{2,1,0:T(8,128)(2,1)}, u32[]{:S(2)}, u32[]{:S(2)}) async-start(bf16[128,14,2048]{2,1,0:T(8,128)(2,1)} %bitcast.183), calls=%async_computation.1 | async-start | bytes 16777216 | tf_op jit(solution)/shard_map/all_to_all | solution.py:214
  245.0 5.5 fusion.132
  250.5 9.4 %convolution_convert_fusion.1 = bf16[1024,2048]{1,0:T(8,128)(2,1)} fusion(bf16[352,2048]{1,0:T(8,128)(2,1)} %param.42, bf16[1024,2048]{1,0:T(8,128)(2,1)} %copy-done.11, bf16[2048,352]{0,1:T(8,128)(2,1)} %param.41, f32[1024,352]{0,1:T(8,128)} %fusion.132), kind=kOutput, calls=%fused_computation.73 | convolution fusion | flops 2957049856 | bytes 12713984 | tf_op jit(solution)/shard_map/dot_general | solution.py:182
  259.9 101.0 %all-to-all-done = bf16[128,14,2048]{2,1,0:T(8,128)(2,1)} async-done(((bf16[128,14,2048]{2,1,0:T(8,128)(2,1)}), bf16[128,14,2048]{2,1,0:T(8,128)(2,1)}, u32[]{:S(2)}, u32[]{:S(2)}) %all-to-all-start) | async-done | bytes 7340064 | tf_op jit(solution)/shard_map/all_to_all | solution.py:214
  360.9 16.0 %fusion.41 = f32[128,14,704]{0,2,1:T(8,128)S(1)} fusion(bf16[128,14,2048]{2,1,0:T(8,128)(2,1)} %all-to-all-done, bf16[1,2048,704]{1,2,0:T(8,128)(2,1)} %param.44), kind=kOutput, calls=%fused_computation.61 | convolution fusion | flops 5167382528 | bytes 15269888 | tf_op jit(solution)/shard_map/pjcd,jdf->pjcf/dot_general | solution.py:219
  377.0 13.6 %fusion.43 = f32[128,14,704]{0,2,1:T(8,128)S(1)} fusion(bf16[128,14,2048]{2,1,0:T(8,128)(2,1)} %all-to-all-done, bf16[1,2048,704]{1,2,0:T(8,128)(2,1)S(1)} %copy-done.30), kind=kOutput, calls=%fused_computation.63 | convolution fusion | flops 5167382528 | bytes 15269888 | tf_op jit(solution)/shard_map/pjcd,jdf->pjcf/dot_general | solution.py:216
  390.6 8.3 %convolution_convert_fusion = bf16[128,14,2048]{2,0,1:T(8,128)(2,1)} fusion(bf16[1,704,2048]{2,1,0:T(8,128)(2,1)S(1)} %copy-done, f32[128,14,704]{0,2,1:T(8,128)S(1)} %fusion.41, f32[128,14,704]{0,2,1:T(8,128)S(1)} %fusion.43), kind=kOutput, calls=%fused_computation.72 | convolution fusion | flops 5178621952 | bytes 20316160 | tf_op jit(solution)/shard_map/pjcf,jfd->pjcd/dot_general | solution.py:221
  399.0 10.4 %copy.99 = bf16[128,14,2048]{2,1,0:T(8,128)(2,1)} copy(bf16[128,14,2048]{2,0,1:T(8,128)(2,1)} %convolution_convert_fusion) | data formatting | bytes 14680064 | tf_op jit(solution)/shard_map/convert_element_type | solution.py:225
  409.3 8.4 %all-to-all-start.1 = ((bf16[128,14,2048]{2,1,0:T(8,128)(2,1)}), bf16[128,14,2048]{2,1,0:T(8,128)(2,1)}, u32[]{:S(2)}, u32[]{:S(2)}) async-start(bf16[128,14,2048]{2,1,0:T(8,128)(2,1)} %copy.99), calls=%async_computation.2 | async-start | bytes 16777216 | tf_op jit(solution)/shard_map/all_to_all | solution.py:224
  417.7 1.2 fusion.133
  419.2 103.0 %all-to-all-done.1 = bf16[128,14,2048]{2,1,0:T(8,128)(2,1)} async-done(((bf16[128,14,2048]{2,1,0:T(8,128)(2,1)}), bf16[128,14,2048]{2,1,0:T(8,128)(2,1)}, u32[]{:S(2)}, u32[]{:S(2)}) %all-to-all-start.1) | async-done | bytes 7340064 | tf_op jit(solution)/shard_map/all_to_all | solution.py:224
  522.2 9.0 %bitcast_reduce_fusion = bf16[64,14,2048]{2,1,0:T(8,128)(2,1)} fusion(bf16[128,14,2048]{2,1,0:T(8,128)(2,1)} %all-to-all-done.1), kind=kLoop, calls=%fused_computation.59 | loop fusion | flops 1835008 | bytes 11010048 | tf_op jit(solution)/shard_map/reduce_sum | solution.py:228
  531.2 5.9 %convert_element_type.152 = bf16[896,2048]{1,0:T(8,128)(2,1)} reshape(bf16[64,14,2048]{2,1,0:T(8,128)(2,1)} %bitcast_reduce_fusion) | data formatting | bytes 7340032 | tf_op jit(solution)/shard_map/convert_element_type | solution.py:230
  537.1 9.6 %gather_fusion.1 = bf16[768,2048]{1,0:T(8,128)(2,1)} fusion(bf16[896,2048]{1,0:T(8,128)(2,1)} %convert_element_type.152, s32[1024]{0:T(1024)S(1)} %pad_clamp_fusion), kind=kCustom, calls=%fused_computation.1 | custom fusion | bytes 6294528 | tf_op jit(solution)/shard_map/gather | solution.py:232
  546.7 6.6 %reshape.334 = f32[128,6,2048]{2,1,0:T(8,128)} reshape(bf16[768,2048]{1,0:T(8,128)(2,1)} %gather_fusion.1) | data formatting | bytes 9437184 | tf_op jit(solution)/shard_map/convert_element_type | solution.py:233
  553.3 7.6 %multiply_reduce_fusion = f32[128,2048]{1,0:T(8,128)} fusion(f32[128,6,2048]{2,1,0:T(8,128)} %reshape.334, f32[128,6]{1,0:T(8,128)S(1)} %copy.92), kind=kLoop, calls=%fused_computation.60 | loop fusion | flops 2883584 | bytes 7343104 | tf_op jit(solution)/shard_map/reduce_sum | solution.py:233
  560.9 2.5 add_convert_fusion
  (117 shorter events, 11.4 us)
Async XLA Ops:
  6.5 384.1 %copy-start = (bf16[1,704,2048]{2,1,0:T(8,128)(2,1)S(1)}, bf16[1,704,2048]{2,1,0:T(8,128)(2,1)}, u32[]{:S(2)}) copy-start(bf16[1,704,2048]{2,1,0:T(8,128)(2,1)} %param.45) | copy-start | bytes 8650756
  6.5 70.6 %all-gather.2.cloned.1.call-start = ((), (), s32[]{:S(2)}) async-start(), calls=%async_computation.3 | async-start | bytes 1179648 | tf_op jit(solution)/shard_map/all_gather | solution.py:146
  6.5 3.3 copy-start.26
  9.8 5.3 copy-start.14
  13.2 1.9 copy-start.9
  15.1 0.7 copy-start.28
  16.5 188.7 %all-reduce.3.cloned.1.call-start = ((), (), s32[]{:S(2)}) async-start(), calls=%async_computation.4 | async-start | bytes 8388608 | tf_op jit(solution)/shard_map/psum | solution.py:174
  17.3 8.5 %copy-start.29 = (f32[32]{0:T(128)}, f32[32]{0:T(128)S(1)}, u32[]{:S(2)}) copy-start(f32[32]{0:T(128)S(1)} %multiply_exponential_fusion) | copy-start | bytes 388
  17.3 4.6 copy-start.24
  21.9 1.1 copy-start.19
  23.0 1.3 copy-start.7
  25.8 4.0 copy-start.6
  29.8 3.9 copy-start.3
  34.5 1.4 copy-start.4
  37.5 3.7 copy-start.1
  42.0 1.3 copy-start.2
  43.3 28.5 %copy-start.10 = (bf16[512,2,64]{0,2,1:T(8,128)(2,1)S(1)}, bf16[512,2,64]{0,2,1:T(8,128)(2,1)}, u32[]{:S(2)}) copy-start(bf16[512,2,64]{0,2,1:T(8,128)(2,1)} %get-tuple-element.435) | copy-start | bytes 393220
  45.8 42.7 %copy-start.20 = (bf16[512,256]{0,1:T(8,128)(2,1)}, bf16[512,256]{0,1:T(8,128)(2,1)S(1)}, u32[]{:S(2)}) copy-start(bf16[512,256]{0,1:T(8,128)(2,1)S(1)} %copy.108) | copy-start | bytes 786436
  77.2 4.5 copy-start.18
  77.2 4.5 copy-start.22
  77.2 4.5 copy-start.23
  80.3 1.4 copy-start.15
  80.3 2.3 copy-start.8
  82.6 1.6 copy-start.17
  82.6 1.6 copy-start.21
  85.1 1.3 copy-start.16
  100.9 0.7 copy-start.25
  107.9 102.8 %copy-start.27 = (f32[2048]{0:T(1024)S(1)}, f32[2048]{0:T(1024)}, u32[]{:S(2)}) copy-start(f32[2048]{0:T(1024)} %param.37) | copy-start | bytes 24580
  210.7 1.9 copy-start.5
  212.6 2.0 copy-start.11
  214.6 0.8 copy-start.12
  233.2 127.7 %all-to-all-start = ((bf16[128,14,2048]{2,1,0:T(8,128)(2,1)}), bf16[128,14,2048]{2,1,0:T(8,128)(2,1)}, u32[]{:S(2)}, u32[]{:S(2)}) async-start(bf16[128,14,2048]{2,1,0:T(8,128)(2,1)} %bitcast.183), calls=%async_computation.1 | async-start | bytes 16777216 | tf_op jit(solution)/shard_map/all_to_all | solution.py:214
  244.5 316.3 %reduce-scatter.2.cloned.1.call-start = ((), (), s32[]{:S(2)}) async-start(), calls=%async_computation.5 | async-start | bytes 4718592 | tf_op jit(solution)/shard_map/reduce_scatter | solution.py:181
  360.9 16.0 %copy-start.30 = (bf16[1,2048,704]{1,2,0:T(8,128)(2,1)S(1)}, bf16[1,2048,704]{1,2,0:T(8,128)(2,1)}, u32[]{:S(2)}) copy-start(bf16[1,2048,704]{1,2,0:T(8,128)(2,1)} %param.43) | copy-start | bytes 8650756
  409.3 8.4 %copy-start.13 = (bf16[128,2048]{1,0:T(8,128)(2,1)S(1)}, bf16[128,2048]{1,0:T(8,128)(2,1)}, u32[]{:S(2)}) copy-start(bf16[128,2048]{1,0:T(8,128)(2,1)} %copy-done.12) | copy-start | bytes 1572868
  409.3 112.8 %all-to-all-start.1 = ((bf16[128,14,2048]{2,1,0:T(8,128)(2,1)}), bf16[128,14,2048]{2,1,0:T(8,128)(2,1)}, u32[]{:S(2)}, u32[]{:S(2)}) async-start(bf16[128,14,2048]{2,1,0:T(8,128)(2,1)} %copy.99), calls=%async_computation.2 | async-start | bytes 16777216 | tf_op jit(solution)/shard_map/all_to_all | solution.py:224
Sparse Core Ops, SparseCore 0:
  16.7 23.8 all-gather.1
  101.0 104.1 all-reduce.2
  260.0 92.2 reduce-scatter.1
where the time goes:
time: 579 us; the launch traced here: 570 us
  waiting for transfers between devices  301 us (52%)
  matrix products  93.4 us (16%)
  local copies, waits for them, and re-layouts  74.6 us (13%)
  other arithmetic  42.8 us (7%)
  blocking collectives  23.3 us (4%)
  starting transfers between devices  20.2 us (3%)
  between operations  14.7 us (3%)
    all_to_all x1, waiting for transfers between devices, per_device(): lax.all_to_all(partial_value.astype(jnp.bfloat16), ('req', 'head'), split...  103 us
    all_to_all x1, waiting for transfers between devices, per_device(): lax.all_to_all(outgoing, ('req', 'head'), split_axis=0, concat_axis=0, ti...  101 us
    psum x1, waiting for transfers between devices, per_device(): lax.psum(attn_term.astype(jnp.bfloat16), 'head').astype(jnp.float32)  97.3 us
    all_gather x1, blocking collectives, per_device(): lax.all_gather(own_rope, 'head', axis=0, tiled=True)  23.3 us
    dot_general x1, matrix products, per_device(): jnp.einsum('pjcd,jdf->pjcf', received, expert_up, preferred_element_type=...  16 us
    dot_general x1, matrix products, per_device(): jnp.einsum('pjcd,jdf->pjcf', received, expert_gate, preferred_element_typ...  13.6 us
  transfers between devices with their start and end apart: 5, of which 3 were waited for; matrix products, arithmetic and copies ran while one was open for 25% of the time, Pallas kernels for 0%

commit v1 on v0

--- a/solution.py
+++ b/solution.py
@@ -125,7 +125,10 @@
     top_count = routes.shape[1]
     head_local = w_query.shape[1] // (NOPE + ROPE)
     length = cache_lengths[0]
-    head_index = lax.axis_index("head")
+    chip_count = lax.axis_size("hx")
+    core_count = lax.axis_size("hc")
+    chip_index = lax.axis_index("hx")
+    core_index = lax.axis_index("hc")
     normed_in = rms_scale(hidden_in.astype(jnp.float32), attn_gain).astype(jnp.bfloat16)
     positions = length + jnp.arange(request_rows, dtype=jnp.int32)
     query_all = jnp.dot(normed_in, w_query, preferred_element_type=jnp.float32).reshape(
@@ -133,19 +136,12 @@
     )
     query_nope = query_all[..., :NOPE].astype(jnp.bfloat16)
     query_rope = rotate(query_all[..., NOPE:], positions).astype(jnp.bfloat16)
-    own_start = head_index * row_count
-    own_in = lax.dynamic_slice_in_dim(normed_in, own_start, row_count, 0)
-    own_positions = length + own_start + jnp.arange(row_count, dtype=jnp.int32)
-    own_latent = rms_scale(
-        jnp.dot(own_in, w_latent, preferred_element_type=jnp.float32), latent_gain
-    ).astype(jnp.bfloat16)
-    own_rope = rotate(
-        jnp.dot(own_in, w_latent_rope, preferred_element_type=jnp.float32), own_positions
-    ).astype(jnp.bfloat16)
-    new_latent, new_rope = (
-        lax.all_gather(own_latent, "head", axis=0, tiled=True),
-        lax.all_gather(own_rope, "head", axis=0, tiled=True),
-    )
+    new_latent = rms_scale(
+        jnp.dot(normed_in, w_latent, preferred_element_type=jnp.float32), latent_gain
+    ).astype(jnp.bfloat16)
+    new_rope = rotate(
+        jnp.dot(normed_in, w_latent_rope, preferred_element_type=jnp.float32), positions
+    ).astype(jnp.bfloat16)
     key_up = w_key_up.reshape(LATENT, head_local, NOPE)
     absorbed = jnp.einsum(
         "chn,lhn->chl", query_nope, key_up, preferred_element_type=jnp.float32
@@ -170,29 +166,37 @@
         ).astype(jnp.bfloat16)
         outputs.append(head_out.reshape(block_rows, head_local * VDIM))
     head_rows = jnp.concatenate(outputs, axis=0)
-    attn_term = jnp.dot(head_rows, w_out, preferred_element_type=jnp.float32)
-    attn_sum = lax.psum(attn_term.astype(jnp.bfloat16), "head").astype(jnp.float32)
-    residual = (hidden_in.astype(jnp.float32) + attn_sum).astype(jnp.bfloat16)
+    def core_major(values):
+        return (
+            values.reshape(chip_count, core_count, row_count, -1)
+            .transpose(1, 0, 2, 3)
+            .reshape(request_rows, -1)
+        )
+
+    head_perm = core_major(head_rows)
+    attn_term = jnp.dot(head_perm, w_out, preferred_element_type=jnp.float32).astype(jnp.bfloat16)
+    attn_half = lax.psum_scatter(
+        attn_term.astype(jnp.float32), "hc", scatter_dimension=0, tiled=True
+    ).astype(jnp.bfloat16)
+    attn_half = lax.psum(attn_half, "hx")
+    attn_sum = lax.all_gather(attn_half, "hc", axis=0, tiled=True).astype(jnp.float32)
+    residual = (core_major(hidden_in).astype(jnp.float32) + attn_sum).astype(jnp.bfloat16)
     normed = rms_scale(residual.astype(jnp.float32), post_gain).astype(jnp.bfloat16)
     shared_act = (
         jax.nn.silu(jnp.dot(normed, shared_gate, preferred_element_type=jnp.float32))
         * jnp.dot(normed, shared_up, preferred_element_type=jnp.float32)
     ).astype(jnp.bfloat16)
+    shared_part = jnp.dot(shared_act, shared_down, preferred_element_type=jnp.float32)
+    shared_core = lax.psum_scatter(shared_part, "hc", scatter_dimension=0, tiled=True)
     shared_own = lax.psum_scatter(
-        jnp.dot(shared_act, shared_down, preferred_element_type=jnp.float32).astype(jnp.bfloat16),
-        "head",
-        scatter_dimension=0,
-        tiled=True,
+        shared_core.astype(jnp.bfloat16), "hx", scatter_dimension=0, tiled=True
     ).astype(jnp.float32)
+    own_start = (core_index * chip_count + chip_index) * row_count
     residual_own = lax.dynamic_slice_in_dim(residual, own_start, row_count, 0)
     normed_own = lax.dynamic_slice_in_dim(normed, own_start, row_count, 0)
     experts = EXPERTS
     capacity = CAP
-    devices = lax.axis_size("req") * lax.axis_size("head")
-    split_count = max(1, devices // experts)
-    local_count = max(1, experts // devices)
-    group_count = devices // split_count
-    slot_width = local_count * capacity
+    slot_total = experts * capacity
     logits = jnp.dot(normed_own, w_router, preferred_element_type=jnp.float32)
     matches = routes[:, :, None] == jnp.arange(experts, dtype=jnp.int32)[None, None, :]
     chosen = jnp.sum(jnp.where(matches, logits[:, None, :], 0.0), axis=-1)
@@ -200,65 +204,83 @@
     pair_hits = matches.reshape(row_count * top_count, experts).astype(jnp.int32)
     pair_ranks = jnp.cumsum(pair_hits, axis=0) - pair_hits
     slot_of = jnp.sum(pair_ranks * pair_hits, axis=-1)
-    target = routes.reshape(-1) * capacity + slot_of
-    slot_token = (
-        jnp.full((experts * capacity,), row_count, jnp.int32)
-        .at[target]
-        .set(jnp.arange(row_count * top_count, dtype=jnp.int32) // top_count)
-    )
-    padded = jnp.concatenate([normed_own, jnp.zeros((1, model_width), jnp.bfloat16)], axis=0)
-    send_rows = padded[slot_token]
-    outgoing = jnp.repeat(
-        send_rows.reshape(group_count, slot_width, model_width), split_count, axis=0
-    )
-    arrived = lax.all_to_all(outgoing, ("req", "head"), split_axis=0, concat_axis=0, tiled=True)
-    received = arrived.reshape(devices, local_count, capacity, model_width)
-    gate_values = jnp.einsum(
-        "pjcd,jdf->pjcf", received, expert_gate, preferred_element_type=jnp.float32
-    )
-    upward = jnp.einsum("pjcd,jdf->pjcf", received, expert_up, preferred_element_type=jnp.float32)
-    activation = (jax.nn.silu(gate_values) * upward).astype(jnp.bfloat16)
-    partial_value = jnp.einsum(
-        "pjcf,jfd->pjcd", activation, expert_down, preferred_element_type=jnp.float32
-    ).reshape(devices, slot_width, model_width)
+    target = (routes.reshape(-1) * capacity + slot_of).reshape(row_count, top_count)
+    slot_ids = jnp.arange(slot_total, dtype=jnp.int32)
+    hit = target[:, :, None] == slot_ids[None, None, :]
+    dispatch = jnp.any(hit, axis=1).astype(jnp.bfloat16)
+    send_rows = jnp.einsum(
+        "ts,td->sd", dispatch, normed_own, preferred_element_type=jnp.float32
+    ).astype(jnp.bfloat16)
+    devices = lax.axis_size(("req", "hx", "hc"))
+    piece = slot_total // devices
+    outgoing = send_rows.reshape(devices, piece, model_width)
+    arrived = lax.all_to_all(
+        outgoing, ("req", "hx", "hc"), split_axis=0, concat_axis=0, tiled=True
+    ).reshape(devices * piece, model_width)
+    swap = [(0, 1), (1, 0)]
+    partner = lax.ppermute(arrived, "hc", swap)
+
+    def expert_part(rows):
+        gate_values = jnp.dot(rows, expert_gate[0], preferred_element_type=jnp.float32)
+        upward = jnp.dot(rows, expert_up[0], preferred_element_type=jnp.float32)
+        activation = (jax.nn.silu(gate_values) * upward).astype(jnp.bfloat16)
+        return jnp.dot(activation, expert_down[0], preferred_element_type=jnp.float32)
+
+    own_part = expert_part(arrived)
+    partner_part = expert_part(partner)
+    partner_back = lax.ppermute(partner_part.astype(jnp.bfloat16), "hc", swap)
+    expert_done = (own_part + partner_back.astype(jnp.float32)).astype(jnp.bfloat16)
     returned = lax.all_to_all(
-        partial_value.astype(jnp.bfloat16), ("req", "head"), split_axis=0, concat_axis=0, tiled=True
-    ).astype(partial_value.dtype)
-    expert_rows = (
-        jnp.sum(returned.reshape(group_count, split_count, slot_width, model_width), axis=1)
-        .reshape(experts * capacity, model_width)
-        .astype(jnp.bfloat16)
-    )
-    picked = expert_rows[target].reshape(row_count, top_count, model_width)
-    routed = jnp.sum(route_weight[:, :, None] * picked, axis=1)
+        expert_done.reshape(devices, piece, model_width),
+        ("req", "hx", "hc"),
+        split_axis=0,
+        concat_axis=0,
+        tiled=True,
+    ).reshape(slot_total, model_width)
+    combine = jnp.sum(jnp.where(hit, route_weight[:, :, None], 0.0), axis=1)
+    routed = jnp.dot(
+        combine,
+        returned.astype(jnp.float32),
+        precision=lax.Precision.HIGHEST,
+        preferred_element_type=jnp.float32,
+    )
     return (residual_own.astype(jnp.float32) + shared_own + routed).astype(jnp.bfloat16)
 
 
 def solution(mesh):
+    core_count = 2
+    split_mesh = jax.sharding.Mesh(
+        mesh.devices.reshape(
+            mesh.shape["req"], mesh.shape["head"] // core_count, core_count
+        ),
+        ("req", "hx", "hc"),
+    )
+    head = ("hx", "hc")
+    every = ("req", "hx", "hc")
     in_specs = (
         P("req", None),
         P("req", None, None),
         P("req", None, None),
         P("req"),
         P(),
-        P(None, "head"),
-        P(),
-        P(),
-        P(),
-        P(None, "head"),
-        P(None, "head"),
-        P("head", None),
-        P(),
-        P(),
-        P(("req", "head"), None),
-        P(None, "head"),
-        P(None, "head"),
-        P("head", None),
-        P(("req", "head"), None, None),
-        P(("req", "head"), None, None),
-        P(("req", "head"), None, None),
-    )
-    out_specs = P(("req", "head"), None)
+        P(None, head),
+        P(),
+        P(),
+        P(),
+        P(None, head),
+        P(None, head),
+        P(head, None),
+        P(),
+        P(),
+        P(every, None),
+        P(None, head),
+        P(None, head),
+        P(head, None),
+        P(every, None, None),
+        P(every, None, None),
+        P(every, None, None),
+    )
+    out_specs = P(every, None)
     return jax.shard_map(
-        per_device, mesh=mesh, in_specs=in_specs, out_specs=out_specs, check_vma=False
-    )
+        per_device, mesh=split_mesh, in_specs=in_specs, out_specs=out_specs, check_vma=False
+    )

time: 579 us -> 475 us (0.82)
  the two profiles are of different devices: /device:TPU:10 before, /device:TPU:1 now
where the time goes in v1:
time: 475 us; the launch traced here: 465 us
  waiting for transfers between devices  186 us (39%)
  matrix products  113 us (24%)
  blocking collectives  62.1 us (13%)
  local copies, waits for them, and re-layouts  52.9 us (11%)
  other arithmetic  29.1 us (6%)
  between operations  14.7 us (3%)
  starting transfers between devices  6.99 us (1%)
    all_to_all x1, blocking collectives, per_device(): lax.all_to_all(outgoing, ('req', 'hx', 'hc'), split_axis=0, concat_axis=0...  62.1 us
    psum x1, waiting for transfers between devices, per_device(): attn_half = lax.psum(attn_half, 'hx')  59.6 us
    reduce_scatter x1, waiting for transfers between devices, per_device(): lax.psum_scatter(attn_term.astype(jnp.float32), 'hc', scatter_dimension=0...  57.8 us
    all_to_all x1, waiting for transfers between devices, per_device(): lax.all_to_all(expert_done.reshape(devices, piece, model_width), ('req',...  50.8 us
    dot_general x2, matrix products, expert_part(): jnp.dot(activation, expert_down[0], preferred_element_type=jnp.float32)  24.5 us
    dot_general x2, matrix products, expert_part(): upward = jnp.dot(rows, expert_up[0], preferred_element_type=jnp.float32)  14 us
    all_gather x1, waiting for transfers between devices, per_device(): lax.all_gather(attn_half, 'hc', axis=0, tiled=True).astype(jnp.float32)  11.6 us
    dot_general x1, matrix products, per_device(): jnp.dot(shared_act, shared_down, preferred_element_type=jnp.float32)  10.6 us
  transfers between devices with their start and end apart: 8, of which 5 were waited for; matrix products, arithmetic and copies ran while one was open for 18% of the time, Pallas kernels for 0%

profile of v1, /device:TPU:1, one launch (start us, length us, event | category | flops | bytes accessed | tf_op | source)
XLA Modules:
  0.0 465.5 jit_solution(10155304224494186032)
XLA Ops:
  6.6 3.2 multiply_reduce_fusion
  10.2 3.5 fusion.126
  13.7 1.5 fusion.124
  17.2 1.9 fusion.107
  19.1 1.9 fusion.104
  21.7 0.8 copy.144
  22.6 6.9 %multiply_reduce_fusion.1 = (f32[1024]{0:T(1024)S(1)}, f32[1024,512]{0,1:T(8,128)}) fusion(bf16[2048,512]{1,0:T(8,128)(2,1)} %param.31, bf16[1024,2048]{1,0:T(8,128)(2,1)} %param.25, f32[2048]{0:T(1024)S(1)} %copy-done.33, f32[1024]{0:T(1024)S(1)} %add_rsqrt_fusion.2), kind=kOutput, calls=%fused_computation.84 | convolution fusion | flops 2156919808 | bytes 8404992 | tf_op jit(solution)/shard_map/dot_general | solution.py:140
  29.5 2.1 convert_bitcast_fusion
  31.6 1.1 broadcast_compare_fusion
  32.7 3.0 fusion.131
  35.6 1.6 broadcast.235.clone
  37.3 6.3 %while.29 = (s32[]{:T(128)}, f32[512,2]{0,1:T(2,128)S(1)}, f32[512,2]{0,1:T(2,128)S(1)}, f32[512,2,512]{2,0,1:T(8,128)}, s32[]{:T(128)}, /*index=5*/s32[]{:T(128...) while((s32[]{:T(128)}, f32[512,2]{0,1:T(2,128)S(1)}, ...), condition=%wide.region_11.12_spmd, body=%wide.region_8.11_spmd.sunk | while | flops 287312128 | bytes 25117576 | solution.py:82
  37.3 1.1 fusion.193
  39.1 1.7 fusion.194
  40.9 0.8 multiply_add_fusion.14
  41.8 1.3 copy-done.4
  43.6 2.0 multiply_convert_fusion.3
  45.8 2.7 fusion.133
  48.6 1.0 fusion.132
  49.6 2.1 fusion.74
  53.0 5.1 %fusion.66 = bf16[2,512,128]{1,2,0:T(8,128)(2,1)} fusion(bf16[512,2,128]{0,2,1:T(8,128)(2,1)} %bitcast.187, f32[512,2,512]{2,0,1:T(8,128)} %fusion.74, f32[512,2,512]{2,0,1:T(8,128)} %get-tuple-element.118, f32[512,2,512]{0,2,1:T(8,128)} %copy-done.11, f32[512,2]{0,1:T(2,128)S(1)} %get-tuple-element.169, f32[512,2]{0,1:T(2,128)S(1)} %get-tuple-element.172, ...), kind=kOutput, calls=%fused_computation.98 | convolution fusion | flops 675414016 | bytes 7356416 | tf_op jit(solution)/shard_map/qhl,lhv->qhv/dot_general | solution.py:164
  58.1 1.8 copy.120
  59.9 2.6 fusion.109
  62.5 1.6 broadcast.235.clone.1
  64.2 5.9 %while.28 = (s32[]{:T(128)}, f32[512,2]{0,1:T(2,128)S(1)}, f32[512,2]{0,1:T(2,128)S(1)}, f32[512,2,512]{2,0,1:T(8,128)}, s32[]{:T(128)}, /*index=5*/s32[]{:T(128...) while((s32[]{:T(128)}, f32[512,2]{0,1:T(2,128)S(1)}, ...), condition=%wide.region_4.5_spmd, body=%wide.region_1.4_spmd.sunk | while | flops 287312128 | bytes 25117576 | solution.py:82
  64.2 1.1 fusion.185
  65.9 1.7 fusion.186
  68.7 1.3 copy-done.2
  70.0 3.0 fusion.134
  73.1 1.3 copy-done.12
  74.7 4.4 fusion.67
  79.1 1.1 copy.119
  80.3 1.1 copy-done.17
  81.4 4.5 convert_convert_fusion
  86.1 57.8 %reduce-scatter.4.cloned.1.call-done = f32[512,2048]{1,0:T(8,128)} async-done(((f32[1024,2048]{1,0:T(8,128)}), f32[512,2048]{1,0:T(8,128)}) %reduce-scatter.4.cloned.1.call-update) | async-done | bytes 4194320 | tf_op jit(solution)/shard_map/reduce_scatter | solution.py:178
  143.9 3.8 convert_element_type.155
  147.8 59.6 %all-reduce.2.cloned.1.call-done = bf16[512,2048]{1,0:T(8,128)(2,1)} async-done(((bf16[512,2048]{1,0:T(8,128)(2,1)}), bf16[512,2048]{1,0:T(8,128)(2,1)}) %all-reduce.2.cloned.1.call-update) | async-done | bytes 2097168 | tf_op jit(solution)/shard_map/psum | solution.py:181
  207.6 6.6 %copy.105 = f32[4,2,128,2048]{3,2,0,1:T(8,128)} copy(bf16[4,2,128,2048]{3,2,1,0:T(8,128)(2,1)} %bitcast.180) | data formatting | bytes 12582912 | tf_op jit(solution)/shard_map/convert_element_type | solution.py:183
  214.3 11.6 %all-gather.2.cloned.1.call-done = bf16[1024,2048]{1,0:T(8,128)(2,1)} async-done(((bf16[512,2048]{1,0:T(8,128)(2,1)}), bf16[1024,2048]{1,0:T(8,128)(2,1)}) %all-gather.2.cloned.1.call-update) | async-done | bytes 4194320 | tf_op jit(solution)/shard_map/all_gather | solution.py:182
  225.9 5.9 %fusion.34 = (f32[1024]{0:T(1024)S(1)}, bf16[1024,2048]{1,0:T(8,128)(2,1)S(1)}) fusion(bf16[1024,2048]{1,0:T(8,128)(2,1)} %all-gather.2.cloned.1.call-done, f32[4,2,128,2048]{3,2,0,1:T(8,128)} %copy.105), kind=kLoop, calls=%fused_computation.46 | loop fusion | flops 12581888 | bytes 16781312 | tf_op jit(solution)/shard_map/reduce_sum | solution.py:17
  231.9 1.0 fusion.36
  232.9 0.9 copy-done.6
  233.8 2.0 copy-done.13
  235.7 2.8 fusion.135
  238.6 10.6 %fusion.65 = f32[1024,2048]{1,0:T(8,128)} fusion(bf16[352,2048]{1,0:T(8,128)(2,1)} %param.42, bf16[1024,2048]{1,0:T(8,128)(2,1)} %copy-done.13, bf16[2048,352]{0,1:T(8,128)(2,1)} %param.41, f32[1024,352]{0,1:T(8,128)} %fusion.135), kind=kOutput, calls=%fused_computation.97 | convolution fusion | flops 2954952704 | bytes 16908288 | tf_op jit(solution)/shard_map/dot_general | solution.py:189
  250.3 1.8 reduce-window.6
  253.2 4.1 convolution_convert_fusion.1
  257.3 6.2 %reshape.288 = bf16[128,7,2048]{2,1,0:T(8,128)(2,1)} reshape(bf16[896,2048]{1,0:T(8,128)(2,1)} %convolution_convert_fusion.1) | data formatting | bytes 7340032 | tf_op jit(solution)/shard_map/reshape | solution.py:216
  263.5 62.1 %all_to_all.10 = bf16[128,7,2048]{2,1,0:T(8,128)(2,1)} all-to-all(bf16[128,7,2048]{2,1,0:T(8,128)(2,1)} %reshape.288), channel_id=1, replica_groups=mesh['req'=16,'hx'=4,'hc'=2] {'req','hx','hc'}, dimensions={0} | all-to-all | bytes 7340032 | tf_op jit(solution)/shard_map/all_to_all | solution.py:217
  325.7 6.0 %reshape.289 = bf16[896,2048]{1,0:T(8,128)(2,1)} reshape(bf16[128,7,2048]{2,1,0:T(8,128)(2,1)} %all_to_all.10) | data formatting | bytes 7340032 | tf_op jit(solution)/shard_map/reshape | solution.py:219
  331.7 1.2 collective-permute-start
  332.9 6.2 %collective-permute-done = bf16[896,2048]{1,0:T(8,128)(2,1)S(1)} collective-permute-done((bf16[896,2048]{1,0:T(8,128)(2,1)}, bf16[896,2048]{1,0:T(8,128)(2,1)S(1)}, u32[]{:S(2)}, u32[]{:S(2)}) %collective-permute-start) | collective-permute-done | bytes 3670048 | tf_op jit(solution)/shard_map/ppermute | solution.py:221
  339.1 1.9 copy-done.30
  341.0 6.4 %fusion.43 = f32[896,704]{0,1:T(8,128)} fusion(bf16[896,2048]{1,0:T(8,128)(2,1)S(1)} %collective-permute-done, bf16[1,2048,704]{1,2,0:T(8,128)(2,1)} %param.44), kind=kOutput, calls=%fused_computation.60 | convolution fusion | flops 2583691264 | bytes 9076736 | tf_op jit(solution)/shard_map/dot_general | solution.py:225
  347.4 11.7 %convolution_convert_fusion = bf16[896,2048]{1,0:T(8,128)(2,1)} fusion(bf16[1,704,2048]{2,1,0:T(8,128)(2,1)S(1)} %copy-done, f32[896,704]{0,1:T(8,128)} %fusion.43, bf16[896,2048]{1,0:T(8,128)(2,1)} %copy-done.30, bf16[1,2048,704]{1,2,0:T(8,128)(2,1)} %param.43), kind=kOutput, calls=%fused_computation.55 | convolution fusion | flops 5173002240 | bytes 15630336 | tf_op jit(solution)/shard_map/dot_general | solution.py:227
  359.7 7.5 %fusion.45 = f32[896,704]{0,1:T(8,128)} fusion(bf16[896,2048]{1,0:T(8,128)(2,1)} %reshape.289, bf16[1,2048,704]{1,2,0:T(8,128)(2,1)} %param.44), kind=kOutput, calls=%fused_computation.62 | convolution fusion | flops 2583691264 | bytes 9076736 | tf_op jit(solution)/shard_map/dot_general | solution.py:225
  367.3 3.9 convert_element_type.162
  371.2 12.8 %add_convert_fusion = bf16[896,2048]{1,0:T(8,128)(2,1)} fusion(bf16[896,2048]{1,0:T(8,128)(2,1)} %collective-permute-done.1, bf16[1,704,2048]{2,1,0:T(8,128)(2,1)S(1)} %copy-done, f32[896,704]{0,1:T(8,128)} %fusion.45, bf16[896,2048]{1,0:T(8,128)(2,1)} %reshape.289, bf16[1,2048,704]{1,2,0:T(8,128)(2,1)} %param.43), kind=kOutput, calls=%fused_computation.53 | convolution fusion | flops 5176672256 | bytes 19300352 | tf_op jit(solution)/shard_map/dot_general | solution.py:227
  384.0 6.0 %reshape.290 = bf16[128,7,2048]{2,1,0:T(8,128)(2,1)} reshape(bf16[896,2048]{1,0:T(8,128)(2,1)} %add_convert_fusion) | data formatting | bytes 7340032 | tf_op jit(solution)/shard_map/reshape | solution.py:234
  390.0 4.9 %all-to-all-start.1 = ((bf16[128,7,2048]{2,1,0:T(8,128)(2,1)}), bf16[128,7,2048]{2,1,0:T(8,128)(2,1)}, u32[]{:S(2)}, u32[]{:S(2)}) async-start(bf16[128,7,2048]{2,1,0:T(8,128)(2,1)} %reshape.290), calls=%async_computation.4 | async-start | bytes 8388608 | tf_op jit(solution)/shard_map/all_to_all | solution.py:233
  394.9 1.4 fusion.92
  396.7 50.8 %all-to-all-done.1 = bf16[128,7,2048]{2,1,0:T(8,128)(2,1)} async-done(((bf16[128,7,2048]{2,1,0:T(8,128)(2,1)}), bf16[128,7,2048]{2,1,0:T(8,128)(2,1)}, u32[]{:S(2)}, u32[]{:S(2)}) %all-to-all-start.1) | async-done | bytes 3670048 | tf_op jit(solution)/shard_map/all_to_all | solution.py:233
  447.5 6.0 %reshape.291 = bf16[896,2048]{1,0:T(8,128)(2,1)} reshape(bf16[128,7,2048]{2,1,0:T(8,128)(2,1)} %all-to-all-done.1) | data formatting | bytes 7340032 | tf_op jit(solution)/shard_map/reshape | solution.py:239
  453.6 4.9 %fusion.52 = bf16[128,2048]{1,0:T(8,128)(2,1)} fusion(f32[128,896]{1,0:T(8,128)S(1)} %select_reduce_fusion, bf16[896,2048]{1,0:T(8,128)(2,1)} %reshape.291, bf16[128,2048]{1,0:T(8,128)(2,1)} %reduce-scatter.8.cloned.1.call-done, bf16[1024,2048]{1,0:T(8,128)(2,1)} %copy-done.6, s32[]{:T(128)S(6)} %select_n.53), kind=kOutput, calls=%fused_computation.74 | convolution fusion | flops 2819883008 | bytes 5701636 | tf_op jit(solution)/shard_map/dot_general | solution.py:241
  (124 shorter events, 10.3 us)
Async XLA Ops:
  6.5 340.9 %copy-start = (bf16[1,704,2048]{2,1,0:T(8,128)(2,1)S(1)}, bf16[1,704,2048]{2,1,0:T(8,128)(2,1)}, u32[]{:S(2)}) copy-start(bf16[1,704,2048]{2,1,0:T(8,128)(2,1)} %param.45) | copy-start | bytes 8650756
  6.5 137.4 %reduce-scatter.4.cloned.1.call-start = ((), (), s32[]{:S(2)}) async-start(), calls=%async_computation.5 | async-start | bytes 12582912 | tf_op jit(solution)/shard_map/reduce_scatter | solution.py:178
  6.6 3.6 copy-start.7
  6.6 3.6 copy-start.33
  10.2 3.5 copy-start.32
  13.7 2.8 copy-start.15
  16.5 2.6 copy-start.18
  16.5 2.6 copy-start.19
  17.2 4.5 copy-start.23
  22.6 6.9 %copy-start.16 = (f32[1024,384]{0,1:T(8,128)S(1)}, f32[1024,384]{0,1:T(8,128)}, u32[]{:S(2)}) copy-start(f32[1024,384]{0,1:T(8,128)} %copy-done.15) | copy-start | bytes 4718596
  22.6 6.9 %copy-start.26 = (bf16[512,256]{1,0:T(8,128)(2,1)S(1)}, bf16[512,256]{1,0:T(8,128)(2,1)}, u32[]{:S(2)}) copy-start(bf16[512,256]{1,0:T(8,128)(2,1)} %param.34) | copy-start | bytes 786436
  35.6 1.6 copy-start.8
  37.3 6.3 %copy-start.29 = (f32[512]{0:T(512)S(1)}, f32[512]{0:T(512)}, u32[]{:S(2)}) copy-start(f32[512]{0:T(512)} %param.33) | copy-start | bytes 6148
  37.3 3.7 copy-start.3
  41.8 1.4 copy-start.4
  43.6 2.2 copy-start.5
  43.6 2.2 copy-start.21
  45.6 4.0 copy-start.9
  45.8 2.8 copy-start.10
  45.8 2.8 copy-start.20
  49.6 2.2 copy-start.11
  53.0 6.9 %copy-start.14 = (bf16[512,2,64]{0,2,1:T(8,128)(2,1)S(1)}, bf16[512,2,64]{0,2,1:T(8,128)(2,1)}, u32[]{:S(2)}) copy-start(bf16[512,2,64]{0,2,1:T(8,128)(2,1)} %get-tuple-element.391) | copy-start | bytes 393220
  64.2 3.7 copy-start.1
  68.7 1.4 copy-start.2
  73.1 1.4 copy-start.12
  73.1 1.7 copy-start.24
  74.7 5.5 %copy-start.22 = (bf16[512,256]{1,0:T(8,128)(2,1)S(1)}, bf16[512,256]{1,0:T(8,128)(2,1)}, u32[]{:S(2)}) copy-start(bf16[512,256]{1,0:T(8,128)(2,1)} %copy.120) | copy-start | bytes 786436
  80.2 1.2 copy-start.17
  86.0 121.4 %all-reduce.2.cloned.1.call-start = ((), (), s32[]{:S(2)}) async-start(), calls=%async_computation.6 | async-start | bytes 4194304 | tf_op jit(solution)/shard_map/psum | solution.py:181
  147.8 78.1 %all-gather.2.cloned.1.call-start = ((), (), s32[]{:S(2)}) async-start(), calls=%async_computation.7 | async-start | bytes 6291456 | tf_op jit(solution)/shard_map/all_gather | solution.py:182
  207.4 159.8 %reduce-scatter.6.cloned.1.call-start = ((), (), s32[]{:S(2)}) async-start(), calls=%async_computation.8 | async-start | bytes 12582912 | tf_op jit(solution)/shard_map/reduce_scatter | solution.py:190
  214.3 17.6 %copy-start.28 = (f32[2048]{0:T(1024)S(1)}, f32[2048]{0:T(1024)}, u32[]{:S(2)}) copy-start(f32[2048]{0:T(1024)} %param.37) | copy-start | bytes 24580
  231.8 1.9 copy-start.6
  231.9 3.9 copy-start.31
  233.8 2.0 copy-start.13
  249.2 0.7 copy-start.27
  249.2 204.4 %reduce-scatter.8.cloned.1.call-start = ((), (), s32[]{:S(2)}) async-start(), calls=%async_computation.9 | async-start | bytes 2621440 | tf_op jit(solution)/shard_map/reduce_scatter | solution.py:191
  331.7 7.4 %collective-permute-start = (bf16[896,2048]{1,0:T(8,128)(2,1)}, bf16[896,2048]{1,0:T(8,128)(2,1)S(1)}, u32[]{:S(2)}, u32[]{:S(2)}) collective-permute-start(bf16[896,2048]{1,0:T(8,128)(2,1)} %reshape.289), channel_id=1, source_target_pairs={{0,1},{1,0},{2,3},{3,2},{4,5},{5,4},{6,7},{7,6},{8,9},{9,8},{10,11... | collective-permute-start | bytes 11010056 | tf_op jit(solution)/shard_map/ppermute | solution.py:221
  339.1 1.9 copy-start.30
  359.1 12.1 %collective-permute-start.1 = (bf16[896,2048]{1,0:T(8,128)(2,1)}, bf16[896,2048]{1,0:T(8,128)(2,1)}, u32[]{:S(2)}, u32[]{:S(2)}) collective-permute-start(bf16[896,2048]{1,0:T(8,128)(2,1)} %convolution_convert_fusion), channel_id=1, source_target_pairs={{0,1},{1,0},{2,3},{3,2},{4,5},{5,4},{6,7},{7,6},{8,9},{9,8},{10,11... | collective-permute-start | bytes 11010056 | tf_op jit(solution)/shard_map/ppermute | solution.py:231
  390.0 4.9 %copy-start.25 = (bf16[2048,64]{0,1:T(8,128)(2,1)S(1)}, bf16[2048,64]{0,1:T(8,128)(2,1)}, u32[]{:S(2)}) copy-start(bf16[2048,64]{0,1:T(8,128)(2,1)} %param.38) | copy-start | bytes 786436
  390.0 57.6 %all-to-all-start.1 = ((bf16[128,7,2048]{2,1,0:T(8,128)(2,1)}), bf16[128,7,2048]{2,1,0:T(8,128)(2,1)}, u32[]{:S(2)}, u32[]{:S(2)}) async-start(bf16[128,7,2048]{2,1,0:T(8,128)(2,1)} %reshape.290), calls=%async_computation.4 | async-start | bytes 8388608 | tf_op jit(solution)/shard_map/all_to_all | solution.py:233
Sparse Core Ops, SparseCore 0:
  86.1 57.7 reduce-scatter.3
  147.9 59.4 all-reduce.1
  209.1 16.7 all-gather.1
  249.3 20.3 reduce-scatter.5
  371.3 25.3 reduce-scatter.7

commit v2 on v1

--- a/solution.py
+++ b/solution.py
@@ -166,22 +166,23 @@
         ).astype(jnp.bfloat16)
         outputs.append(head_out.reshape(block_rows, head_local * VDIM))
     head_rows = jnp.concatenate(outputs, axis=0)
-    def core_major(values):
-        return (
-            values.reshape(chip_count, core_count, row_count, -1)
-            .transpose(1, 0, 2, 3)
-            .reshape(request_rows, -1)
-        )
-
-    head_perm = core_major(head_rows)
-    attn_term = jnp.dot(head_perm, w_out, preferred_element_type=jnp.float32).astype(jnp.bfloat16)
-    attn_half = lax.psum_scatter(
-        attn_term.astype(jnp.float32), "hc", scatter_dimension=0, tiled=True
-    ).astype(jnp.bfloat16)
-    attn_half = lax.psum(attn_half, "hx")
-    attn_sum = lax.all_gather(attn_half, "hc", axis=0, tiled=True).astype(jnp.float32)
-    residual = (core_major(hidden_in).astype(jnp.float32) + attn_sum).astype(jnp.bfloat16)
-    normed = rms_scale(residual.astype(jnp.float32), post_gain).astype(jnp.bfloat16)
+    head_count = chip_count * core_count
+    head_index = chip_index * core_count + core_index
+    attn_term = jnp.dot(head_rows, w_out, preferred_element_type=jnp.float32).astype(jnp.bfloat16)
+    attn_parts = lax.all_to_all(
+        attn_term.reshape(head_count, row_count, model_width),
+        ("hx", "hc"),
+        split_axis=0,
+        concat_axis=0,
+        tiled=True,
+    )
+    attn_own = jnp.sum(attn_parts.astype(jnp.float32), axis=0)
+    own_start = head_index * row_count
+    hidden_own = lax.dynamic_slice_in_dim(hidden_in, own_start, row_count, 0)
+    residual_own = (hidden_own.astype(jnp.float32) + attn_own).astype(jnp.bfloat16)
+    normed_own = rms_scale(residual_own.astype(jnp.float32), post_gain).astype(jnp.bfloat16)
+    normed_chips = lax.all_gather(normed_own, "hx", axis=0, tiled=True)
+    normed = lax.all_gather(normed_chips, "hc", axis=0, tiled=True)
     shared_act = (
         jax.nn.silu(jnp.dot(normed, shared_gate, preferred_element_type=jnp.float32))
         * jnp.dot(normed, shared_up, preferred_element_type=jnp.float32)
@@ -191,12 +192,8 @@
     shared_own = lax.psum_scatter(
         shared_core.astype(jnp.bfloat16), "hx", scatter_dimension=0, tiled=True
     ).astype(jnp.float32)
-    own_start = (core_index * chip_count + chip_index) * row_count
-    residual_own = lax.dynamic_slice_in_dim(residual, own_start, row_count, 0)
-    normed_own = lax.dynamic_slice_in_dim(normed, own_start, row_count, 0)
     experts = EXPERTS
     capacity = CAP
-    slot_total = experts * capacity
     logits = jnp.dot(normed_own, w_router, preferred_element_type=jnp.float32)
     matches = routes[:, :, None] == jnp.arange(experts, dtype=jnp.int32)[None, None, :]
     chosen = jnp.sum(jnp.where(matches, logits[:, None, :], 0.0), axis=-1)
@@ -205,40 +202,42 @@
     pair_ranks = jnp.cumsum(pair_hits, axis=0) - pair_hits
     slot_of = jnp.sum(pair_ranks * pair_hits, axis=-1)
     target = (routes.reshape(-1) * capacity + slot_of).reshape(row_count, top_count)
-    slot_ids = jnp.arange(slot_total, dtype=jnp.int32)
-    hit = target[:, :, None] == slot_ids[None, None, :]
+    devices = lax.axis_size(("req", "hx", "hc"))
+    piece = experts * capacity // devices
+    dest_ids = jnp.arange(devices, dtype=jnp.int32)[:, None] * piece + jnp.arange(
+        piece, dtype=jnp.int32
+    )[None, :]
+    hit = target[:, :, None, None] == dest_ids[None, None, :, :]
     dispatch = jnp.any(hit, axis=1).astype(jnp.bfloat16)
-    send_rows = jnp.einsum(
-        "ts,td->sd", dispatch, normed_own, preferred_element_type=jnp.float32
-    ).astype(jnp.bfloat16)
-    devices = lax.axis_size(("req", "hx", "hc"))
-    piece = slot_total // devices
-    outgoing = send_rows.reshape(devices, piece, model_width)
+    outgoing = jnp.einsum(
+        "tpj,td->pjd", dispatch, normed_own, preferred_element_type=jnp.float32
+    ).astype(jnp.bfloat16)
     arrived = lax.all_to_all(
         outgoing, ("req", "hx", "hc"), split_axis=0, concat_axis=0, tiled=True
-    ).reshape(devices * piece, model_width)
+    )
     swap = [(0, 1), (1, 0)]
     partner = lax.ppermute(arrived, "hc", swap)
 
     def expert_part(rows):
-        gate_values = jnp.dot(rows, expert_gate[0], preferred_element_type=jnp.float32)
-        upward = jnp.dot(rows, expert_up[0], preferred_element_type=jnp.float32)
+        gate_values = jnp.einsum(
+            "pjd,df->pjf", rows, expert_gate[0], preferred_element_type=jnp.float32
+        )
+        upward = jnp.einsum("pjd,df->pjf", rows, expert_up[0], preferred_element_type=jnp.float32)
         activation = (jax.nn.silu(gate_values) * upward).astype(jnp.bfloat16)
-        return jnp.dot(activation, expert_down[0], preferred_element_type=jnp.float32)
+        return jnp.einsum(
+            "pjf,fd->pjd", activation, expert_down[0], preferred_element_type=jnp.float32
+        )
 
     own_part = expert_part(arrived)
     partner_part = expert_part(partner)
     partner_back = lax.ppermute(partner_part.astype(jnp.bfloat16), "hc", swap)
     expert_done = (own_part + partner_back.astype(jnp.float32)).astype(jnp.bfloat16)
     returned = lax.all_to_all(
-        expert_done.reshape(devices, piece, model_width),
-        ("req", "hx", "hc"),
-        split_axis=0,
-        concat_axis=0,
-        tiled=True,
-    ).reshape(slot_total, model_width)
-    combine = jnp.sum(jnp.where(hit, route_weight[:, :, None], 0.0), axis=1)
-    routed = jnp.dot(
+        expert_done, ("req", "hx", "hc"), split_axis=0, concat_axis=0, tiled=True
+    )
+    combine = jnp.sum(jnp.where(hit, route_weight[:, :, None, None], 0.0), axis=1)
+    routed = jnp.einsum(
+        "tpj,pjd->td",
         combine,
         returned.astype(jnp.float32),
         precision=lax.Precision.HIGHEST,

time: 475 us -> 456 us (0.960)
  waiting for transfers between devices: 186 us -> 154 us
  matrix products: 113 us -> 131 us
  local copies, waits for them, and re-layouts: 52.9 us -> 38.8 us
  starting transfers between devices: 6.99 us -> 12.9 us
    psum x1 -> x0, waiting for transfers between devices: 59.6 us -> none  [per_device(): attn_half = lax.psum(attn_half, 'hx')]
    reduce_scatter x1 -> x0, waiting for transfers between devices: 57.8 us -> none  [per_device(): lax.psum_scatter(attn_term.astype(jnp.float32), 'hc', scatter_dimension=0...]
    all_to_all x1 -> x2, waiting for transfers between devices: 50.8 us -> 99.7 us  [the longest x1 50.9 us: per_device(): lax.all_to_all(expert_done, ('req', 'hx', 'hc'), split_axis=0, concat_axi...]
    all_gather x1 -> x2, waiting for transfers between devices: 11.6 us -> 48 us  [the longest x1 29.8 us: per_device(): normed_chips = lax.all_gather(normed_own, 'hx', axis=0, tiled=True)]
    reshape x6 -> x0, local copies, waits for them, and re-layouts: 27.2 us -> none  [the longest x1 6.23 us: per_device(): outgoing = send_rows.reshape(devices, piece, model_width)]
    dot_general x5 -> x11, matrix products: 10.2 us -> 18.7 us  [update(): jnp.einsum('qhl,kl->qhk', absorbed, keys_latent, preferred_element_type=j...]
    while x10 -> x40, local copies, waits for them, and re-layouts: 2.71 us -> 11.2 us
    dot_general x5 -> x11, matrix products: 8.59 us -> 15.1 us  [update(): jnp.einsum('qhr,kr->qhk', query_rope, keys_rope, preferred_element_type=j...]
  transfers between devices with their start and end apart: 8 -> 8, of which waited for: 5 -> 5; matrix products, arithmetic and copies ran while one was open for 18% -> 14% of each run, Pallas kernels for 0% -> 0%
where the time goes in v2:
time: 456 us; the launch traced here: 447 us
  waiting for transfers between devices  154 us (34%)
  matrix products  131 us (29%)
  blocking collectives  62.1 us (14%)
  local copies, waits for them, and re-layouts  38.8 us (9%)
  other arithmetic  32.8 us (7%)
  between operations  14.8 us (3%)
  starting transfers between devices  12.9 us (3%)
    all_to_all x1, blocking collectives, per_device(): lax.all_to_all(outgoing, ('req', 'hx', 'hc'), split_axis=0, concat_axis=0...  62.1 us
    all_to_all x1, waiting for transfers between devices, per_device(): lax.all_to_all(expert_done, ('req', 'hx', 'hc'), split_axis=0, concat_axi...  50.9 us
    all_to_all x1, waiting for transfers between devices, per_device(): lax.all_to_all(attn_term.reshape(head_count, row_count, model_width), ('h...  48.8 us
    all_gather x1, waiting for transfers between devices, per_device(): normed_chips = lax.all_gather(normed_own, 'hx', axis=0, tiled=True)  29.8 us
    dot_general x2, matrix products, expert_part(): jnp.einsum('pjf,fd->pjd', activation, expert_down[0], preferred_element_t...  24.2 us
    dot_general x11, matrix products, update(): jnp.einsum('qhl,kl->qhk', absorbed, keys_latent, preferred_element_type=j...  18.7 us
    all_gather x1, waiting for transfers between devices, per_device(): normed = lax.all_gather(normed_chips, 'hc', axis=0, tiled=True)  18.2 us
    dot_general x11, matrix products, update(): jnp.einsum('qhr,kr->qhk', query_rope, keys_rope, preferred_element_type=j...  15.1 us
  transfers between devices with their start and end apart: 8, of which 5 were waited for; matrix products, arithmetic and copies ran while one was open for 14% of the time, Pallas kernels for 0%

profile of v2, /device:TPU:1, one launch (start us, length us, event | category | flops | bytes accessed | tf_op | source)
XLA Modules:
  0.0 446.6 jit_solution(15621099184180472906)
XLA Ops:
  8.7 3.2 fusion.34
  12.2 1.5 fusion.136
  13.7 2.1 fusion.140
  17.2 1.8 fusion.117
  19.0 1.8 fusion.120
  20.8 2.0 convert_bitcast_fusion
  22.8 1.5 fusion.145
  24.8 1.9 fusion.122
  26.7 1.6 broadcast.247.clone.1
  28.3 24.3 %while.28 = (s32[]{:T(128)}, f32[512,2]{0,1:T(2,128)S(1)}, f32[512,2]{0,1:T(2,128)S(1)}, f32[512,2,512]{2,0,1:T(8,128)}, s32[]{:T(128)}, /*index=5*/s32[]{:T(128...) while((s32[]{:T(128)}, f32[512,2]{0,1:T(2,128)S(1)}, ...), condition=%wide.region_4.5_spmd, body=%wide.region_1.4_spmd.sunk | while | flops 287312128 | bytes 25117568 | solution.py:82
  28.3 1.3 fusion.199
  30.3 1.7 fusion.200
  33.0 1.3 copy-done.4
  34.4 1.3 fusion.199
  36.4 1.7 fusion.200
  39.1 1.3 copy-done.4
  40.4 1.3 fusion.199
  42.4 1.7 fusion.200
  45.2 1.3 copy-done.4
  46.5 1.3 fusion.199
  48.5 1.7 fusion.200
  51.2 1.3 copy-done.4
  52.6 6.7 %multiply_reduce_fusion = (f32[1024]{0:T(1024)S(1)}, f32[1024,512]{0,1:T(8,128)}) fusion(bf16[2048,512]{1,0:T(8,128)(2,1)} %param.31, bf16[1024,2048]{1,0:T(8,128)(2,1)} %param.25, f32[2048]{0:T(1024)} %param.29, f32[1024]{0:T(1024)} %copy-done.28), kind=kOutput, calls=%fused_computation.84 | convolution fusion | flops 2156919808 | bytes 8404992 | tf_op jit(solution)/shard_map/dot_general | solution.py:140
  59.8 1.8 copy.151
  61.6 1.7 broadcast.247.clone
  63.4 24.0 %while.29 = (s32[]{:T(128)}, f32[512,2]{0,1:T(2,128)S(1)}, f32[512,2]{0,1:T(2,128)S(1)}, f32[512,2,512]{2,0,1:T(8,128)}, s32[]{:T(128)}, /*index=5*/s32[]{:T(128...) while((s32[]{:T(128)}, f32[512,2]{0,1:T(2,128)S(1)}, ...), condition=%wide.region_11.12_spmd, body=%wide.region_8.11_spmd.sunk | while | flops 287312128 | bytes 25117568 | solution.py:82
  65.3 1.7 fusion.208
  68.1 1.4 copy-done.2
  71.3 1.7 fusion.208
  74.0 1.4 copy-done.2
  77.3 1.7 fusion.208
  80.0 1.4 copy-done.2
  83.2 1.7 fusion.208
  85.9 1.4 copy-done.2
  88.6 1.8 multiply_convert_fusion.2
  90.5 2.9 fusion.148
  98.4 2.1 fusion.86
  101.4 3.6 fusion.80
  105.1 4.4 fusion.79
  109.5 4.5 %convolution_convert_fusion = bf16[1024,2048]{1,0:T(8,128)(2,1)} fusion(bf16[256,2048]{1,0:T(8,128)(2,1)} %param.36, bf16[512,256]{0,1:T(8,128)(2,1)S(1)} %bitcast.185, bf16[512,256]{0,1:T(8,128)(2,1)S(1)} %bitcast.184), kind=kOutput, calls=%fused_computation.51 | convolution fusion | flops 1076887552 | bytes 5767168 | tf_op jit(solution)/shard_map/dot_general | solution.py:171
  114.0 5.8 %all-to-all-start = ((bf16[8,128,2048]{2,1,0:T(8,128)(2,1)}), bf16[8,128,2048]{2,1,0:T(8,128)(2,1)}, u32[]{:S(2)}, u32[]{:S(2)}) async-start(bf16[8,128,2048]{2,1,0:T(8,128)(2,1)} %bitcast.179), calls=%async_computation | async-start | bytes 8388608 | tf_op jit(solution)/shard_map/all_to_all | solution.py:172
  119.8 48.8 %all-to-all-done = bf16[8,128,2048]{2,1,0:T(8,128)(2,1)} async-done(((bf16[8,128,2048]{2,1,0:T(8,128)(2,1)}), bf16[8,128,2048]{2,1,0:T(8,128)(2,1)}, u32[]{:S(2)}, u32[]{:S(2)}) %all-to-all-start) | async-done | bytes 4194336 | tf_op jit(solution)/shard_map/all_to_all | solution.py:172
  168.6 3.0 convert_reduce_fusion
  171.6 1.3 fusion.81
  174.7 29.8 %all-gather.3.cloned.1.call-done = bf16[512,2048]{1,0:T(8,128)(2,1)} async-done(((bf16[128,2048]{1,0:T(8,128)(2,1)}), bf16[512,2048]{1,0:T(8,128)(2,1)}) %all-gather.3.cloned.1.call-update) | async-done | bytes 2097168 | tf_op jit(solution)/shard_map/all_gather | solution.py:184
  205.0 18.2 %all-gather.5.cloned.1.call-done = bf16[1024,2048]{1,0:T(8,128)(2,1)} async-done(((bf16[512,2048]{1,0:T(8,128)(2,1)}), bf16[1024,2048]{1,0:T(8,128)(2,1)}) %all-gather.5.cloned.1.call-update) | async-done | bytes 4194320 | tf_op jit(solution)/shard_map/all_gather | solution.py:185
  223.2 5.4 %fusion.149 = f32[1024,352]{0,1:T(8,128)} fusion(bf16[1024,2048]{1,0:T(8,128)(2,1)} %all-gather.5.cloned.1.call-done, bf16[2048,352]{0,1:T(8,128)(2,1)} %param.40), kind=kOutput, calls=%fused_computation.197 | convolution fusion | flops 1476395008 | bytes 7077888 | tf_op jit(solution)/shard_map/dot_general | solution.py:187
  228.7 10.7 %fusion.78 = f32[1024,2048]{1,0:T(8,128)} fusion(bf16[352,2048]{1,0:T(8,128)(2,1)} %param.42, bf16[1024,2048]{1,0:T(8,128)(2,1)} %all-gather.5.cloned.1.call-done, bf16[2048,352]{0,1:T(8,128)(2,1)} %param.41, f32[1024,352]{0,1:T(8,128)} %fusion.149), kind=kOutput, calls=%fused_computation.100 | convolution fusion | flops 2954952704 | bytes 16908288 | tf_op jit(solution)/shard_map/dot_general | solution.py:190
  241.1 4.4 reduce-window.6
  249.6 2.0 copy.126
  251.6 62.1 %all_to_all.15 = bf16[128,7,2048]{2,1,0:T(8,128)(2,1)S(1)} all-to-all(bf16[128,7,2048]{2,1,0:T(8,128)(2,1)S(1)} %copy.126), channel_id=1, replica_groups=mesh['req'=16,'hx'=4,'hc'=2] {'req','hx','hc'}, dimensions={0} | all-to-all | bytes 7340032 | tf_op jit(solution)/shard_map/all_to_all | solution.py:215
  313.8 2.3 copy.127
  316.1 1.8 copy-done.16
  318.8 6.0 %collective-permute-done = bf16[128,7,2048]{2,0,1:T(8,128)(2,1)S(1)} collective-permute-done((bf16[128,7,2048]{2,0,1:T(8,128)(2,1)S(1)}, bf16[128,7,2048]{2,0,1:T(8,128)(2,1)S(1)}, u32[]{:S(2)}, u32[]{:S(2)}) %collective-permute-start) | collective-permute-done | bytes 3670048 | tf_op jit(solution)/shard_map/ppermute | solution.py:219
  324.8 1.8 copy-done.29
  326.7 4.7 %fusion.44 = f32[128,7,704]{0,2,1:T(8,128)} fusion(bf16[128,7,2048]{2,0,1:T(8,128)(2,1)S(1)} %collective-permute-done, bf16[1,2048,704]{1,2,0:T(8,128)(2,1)S(1)} %copy-done.30), kind=kOutput, calls=%fused_computation.61 | convolution fusion | flops 2583691264 | bytes 9076736 | tf_op jit(solution)/shard_map/pjd,df->pjf/dot_general | solution.py:225
  331.4 11.6 %convolution_convert_fusion.1 = bf16[128,7,2048]{2,0,1:T(8,128)(2,1)} fusion(bf16[1,704,2048]{2,1,0:T(8,128)(2,1)S(1)} %copy-done, f32[128,7,704]{0,2,1:T(8,128)} %fusion.44, bf16[128,7,2048]{2,0,1:T(8,128)(2,1)} %copy-done.29, bf16[1,2048,704]{1,2,0:T(8,128)(2,1)} %param.43), kind=kOutput, calls=%fused_computation.54 | convolution fusion | flops 5173002240 | bytes 15630336 | tf_op jit(solution)/shard_map/pjf,fd->pjd/dot_general | solution.py:227
  343.5 6.9 %fusion.46 = f32[128,7,704]{0,2,1:T(8,128)} fusion(bf16[128,7,2048]{2,0,1:T(8,128)(2,1)} %copy-done.16, bf16[1,2048,704]{1,2,0:T(8,128)(2,1)} %param.44), kind=kOutput, calls=%fused_computation.63 | convolution fusion | flops 2583691264 | bytes 9076736 | tf_op jit(solution)/shard_map/pjd,df->pjf/dot_general | solution.py:225
  350.4 3.9 convert_element_type.139
  354.3 12.6 %add_convert_fusion = bf16[128,7,2048]{2,0,1:T(8,128)(2,1)} fusion(bf16[128,7,2048]{2,0,1:T(8,128)(2,1)} %collective-permute-done.1, bf16[1,704,2048]{2,1,0:T(8,128)(2,1)S(1)} %copy-done, f32[128,7,704]{0,2,1:T(8,128)} %fusion.46, bf16[128,7,2048]{2,0,1:T(8,128)(2,1)} %copy-done.16, bf16[1,2048,704]{1,2,0:T(8,128)(2,1)} %param.43), kind=kOutput, calls=%fused_computation.50 | convolution fusion | flops 5176672256 | bytes 19300352 | tf_op jit(solution)/shard_map/pjf,fd->pjd/dot_general | solution.py:227
  367.0 6.2 %copy.130 = bf16[128,7,2048]{2,1,0:T(8,128)(2,1)} copy(bf16[128,7,2048]{2,0,1:T(8,128)(2,1)} %add_convert_fusion) | data formatting | bytes 7340032 | tf_op jit(solution)/shard_map/convert_element_type | solution.py:234
  373.2 5.1 %all-to-all-start.2 = ((bf16[128,7,2048]{2,1,0:T(8,128)(2,1)}), bf16[128,7,2048]{2,1,0:T(8,128)(2,1)}, u32[]{:S(2)}, u32[]{:S(2)}) async-start(bf16[128,7,2048]{2,1,0:T(8,128)(2,1)} %copy.130), calls=%async_computation.4 | async-start | bytes 8388608 | tf_op jit(solution)/shard_map/all_to_all | solution.py:235
  380.0 50.9 %all-to-all-done.2 = bf16[128,7,2048]{2,1,0:T(8,128)(2,1)} async-done(((bf16[128,7,2048]{2,1,0:T(8,128)(2,1)}), bf16[128,7,2048]{2,1,0:T(8,128)(2,1)}, u32[]{:S(2)}, u32[]{:S(2)}) %all-to-all-start.2) | async-done | bytes 3670048 | tf_op jit(solution)/shard_map/all_to_all | solution.py:235
  430.8 8.8 %fusion.59 = bf16[128,2048]{1,0:T(8,128)(2,1)} fusion(f32[128,128,7]{1,0,2:T(8,128)S(1)} %fusion.52, bf16[128,7,2048]{2,1,0:T(8,128)(2,1)} %all-to-all-done.2, bf16[128,2048]{1,0:T(8,128)(2,1)} %copy-done.17, bf16[128,2048]{1,0:T(8,128)(2,1)} %reduce-scatter.5.cloned.1.call-done), kind=kOutput, calls=%fused_computation.74 | convolution fusion | flops 2819883008 | bytes 5701632 | tf_op jit(solution)/shard_map/tpj,pjd->td/dot_general | solution.py:239
  (191 shorter events, 39.9 us)
Async XLA Ops:
  6.5 324.9 %copy-start = (bf16[1,704,2048]{2,1,0:T(8,128)(2,1)S(1)}, bf16[1,704,2048]{2,1,0:T(8,128)(2,1)}, u32[]{:S(2)}) copy-start(bf16[1,704,2048]{2,1,0:T(8,128)(2,1)} %param.45) | copy-start | bytes 8650756
  7.4 4.6 %copy-start.32 = (bf16[2048,64]{0,1:T(8,128)(2,1)S(1)}, bf16[2048,64]{0,1:T(8,128)(2,1)}, u32[]{:S(2)}) copy-start(bf16[2048,64]{0,1:T(8,128)(2,1)} %param.32) | copy-start | bytes 786436
  8.7 3.4 copy-start.15
  8.7 3.4 copy-start.33
  12.0 1.7 copy-start.28
  12.2 1.5 copy-start.31
  15.8 3.1 copy-start.18
  16.4 2.6 copy-start.19
  16.4 2.6 copy-start.21
  17.2 3.6 copy-start.25
  22.8 2.0 copy-start.5
  22.8 2.0 copy-start.14
  22.8 2.0 copy-start.20
  22.8 2.0 copy-start.22
  24.8 3.5 copy-start.7
  28.3 3.9 copy-start.3
  33.0 1.4 copy-start.4
  34.4 3.8 copy-start.3
  39.1 1.4 copy-start.4
  40.4 3.8 copy-start.3
  45.1 1.4 copy-start.4
  46.5 3.8 copy-start.3
  51.2 1.4 copy-start.4
  63.6 3.7 copy-start.1
  68.1 1.5 copy-start.2
  69.5 3.6 copy-start.1
  74.0 1.5 copy-start.2
  75.5 3.6 copy-start.1
  80.0 1.5 copy-start.2
  81.4 3.6 copy-start.1
  85.9 1.5 copy-start.2
  87.4 3.0 copy-start.6
  87.4 3.1 copy-start.23
  90.5 7.9 %copy-start.8 = (bf16[1024,512]{0,1:T(8,128)(2,1)}, bf16[1024,512]{0,1:T(8,128)(2,1)S(1)}, u32[]{:S(2)}) copy-start(bf16[1024,512]{0,1:T(8,128)(2,1)S(1)} %multiply_convert_fusion.2) | copy-start | bytes 3145732
  93.4 1.4 copy-start.12
  93.4 2.3 copy-start.11
  95.7 1.6 copy-start.10
  96.7 3.7 copy-start.13
  100.5 1.0 copy-start.24
  114.0 54.6 %all-to-all-start = ((bf16[8,128,2048]{2,1,0:T(8,128)(2,1)}), bf16[8,128,2048]{2,1,0:T(8,128)(2,1)}, u32[]{:S(2)}, u32[]{:S(2)}) async-start(bf16[8,128,2048]{2,1,0:T(8,128)(2,1)} %bitcast.179), calls=%async_computation | async-start | bytes 8388608 | tf_op jit(solution)/shard_map/all_to_all | solution.py:172
  119.8 84.8 %all-gather.3.cloned.1.call-start = ((), (), s32[]{:S(2)}) async-start(), calls=%async_computation.5 | async-start | bytes 2621440 | tf_op jit(solution)/shard_map/all_gather | solution.py:184
  171.6 2.1 copy-start.27
  172.9 0.8 copy-start.17
  174.7 48.5 %all-gather.5.cloned.1.call-start = ((), (), s32[]{:S(2)}) async-start(), calls=%async_computation.6 | async-start | bytes 6291456 | tf_op jit(solution)/shard_map/all_gather | solution.py:185
  204.6 145.9 %reduce-scatter.3.cloned.1.call-start = ((), (), s32[]{:S(2)}) async-start(), calls=%async_computation.7 | async-start | bytes 12582912 | tf_op jit(solution)/shard_map/reduce_scatter | solution.py:191
  239.4 0.7 copy-start.26
  239.4 9.1 %copy-start.9 = (bf16[128,2048]{1,0:T(8,128)(2,1)S(1)}, bf16[128,2048]{1,0:T(8,128)(2,1)}, u32[]{:S(2)}) copy-start(bf16[128,2048]{1,0:T(8,128)(2,1)} %fusion.83) | copy-start | bytes 1572868
  239.4 191.5 %reduce-scatter.5.cloned.1.call-start = ((), (), s32[]{:S(2)}) async-start(), calls=%async_computation.8 | async-start | bytes 2621440 | tf_op jit(solution)/shard_map/reduce_scatter | solution.py:192
  313.8 12.9 %copy-start.30 = (bf16[1,2048,704]{1,2,0:T(8,128)(2,1)S(1)}, bf16[1,2048,704]{1,2,0:T(8,128)(2,1)}, u32[]{:S(2)}) copy-start(bf16[1,2048,704]{1,2,0:T(8,128)(2,1)} %param.44) | copy-start | bytes 8650756
  316.1 1.8 copy-start.16
  317.9 7.0 %collective-permute-start = (bf16[128,7,2048]{2,0,1:T(8,128)(2,1)S(1)}, bf16[128,7,2048]{2,0,1:T(8,128)(2,1)S(1)}, u32[]{:S(2)}, u32[]{:S(2)}) collective-permute-start(bf16[128,7,2048]{2,0,1:T(8,128)(2,1)S(1)} %copy.127), channel_id=1, source_target_pairs={{0,1},{1,0},{2,3},{3,2},{4,5},{5,4},{6,7},{7,6},{8,9},{9,8},{10,11... | collective-permute-start | bytes 11010056 | tf_op jit(solution)/shard_map/ppermute | solution.py:219
  324.8 1.8 copy-start.29
  343.0 11.3 %collective-permute-start.1 = (bf16[128,7,2048]{2,0,1:T(8,128)(2,1)}, bf16[128,7,2048]{2,0,1:T(8,128)(2,1)}, u32[]{:S(2)}, u32[]{:S(2)}) collective-permute-start(bf16[128,7,2048]{2,0,1:T(8,128)(2,1)} %convolution_convert_fusion.1), channel_id=1, source_target_pairs={{0,1},{1,0},{2,3},{3,2},{4,5},{5,4},{6,7},{7,6},{8,9},{9,8},{10,11... | collective-permute-start | bytes 11010056 | tf_op jit(solution)/shard_map/ppermute | solution.py:233
  373.2 57.7 %all-to-all-start.2 = ((bf16[128,7,2048]{2,1,0:T(8,128)(2,1)}), bf16[128,7,2048]{2,1,0:T(8,128)(2,1)}, u32[]{:S(2)}, u32[]{:S(2)}) async-start(bf16[128,7,2048]{2,1,0:T(8,128)(2,1)} %copy.130), calls=%async_computation.4 | async-start | bytes 8388608 | tf_op jit(solution)/shard_map/all_to_all | solution.py:235
Sparse Core Ops, SparseCore 0:
  174.8 29.6 all-gather.2
  206.2 16.9 all-gather.4
  239.5 20.3 reduce-scatter.2
  354.4 25.2 reduce-scatter.4
